TPU v7x, 32 devices: a whole 2x2x4 slice. The times are simulated.
32 devices in a mesh: visit: 8 (over z, x), sky: 4 (over y, core).
Axes of the slice: x: 2, y: 2, z: 4, core: 2. Of those that a mesh axis runs over, the one named last changes fastest.
Arguments:
- warped: bfloat16 [16, 512, 2048], P('visit', 'sky'), may hold values from -11 to 21
- inv_var: bfloat16 [16, 512, 2048], P('visit', 'sky'), may hold values from 0.19921875 to 5
- intersection: int32 [8, 4, 4], P('visit', 'sky'), may hold values from 0 to 3, as said below
- col_start: int32 [8, 4], P('visit', 'sky'), may hold values from 0 to 1536, as said below
- row_interp: bfloat16 [8, 4, 512, 512], P('visit', 'sky'), may hold values from -0.22 to 1.4, as said below
- col_interp: bfloat16 [8, 4, 512, 512], P('visit', 'sky'), may hold values from -0.22 to 1.4, as said below
- cell_ids: int32 [8, 4, 4, 4], P('visit', 'sky'), may hold values from 0 to 15
- kernels: bfloat16 [8, 4, 16, 121], P('visit', 'sky'), may hold values from -0.59765625 to 0.59765625
- science: bfloat16 [8, 4, 512, 512], P('visit', 'sky'), may hold values from -8 to 8
- inv_sigma: bfloat16 [8, 4, 512, 512], P('visit', 'sky'), may hold values from 0.29882812 to 1
Outputs:
- coadd: float32 [512, 2048], P('sky')
- outlier_weight: float32 [8, 4, 512, 512], P('visit', 'sky')
Inputs may be any that keep to these rules, and one draw needn't show every extreme that they name: `intersection`: the 4 strip numbers of one tile are distinct. `col_start`: a multiple of 128. `row_interp`: nonzero only within two places of the diagonal, each row's diagonal entry larger than the sum of its other magnitudes. `col_interp`: nonzero only within two places of the diagonal, each row's diagonal entry larger than the sum of its other magnitudes.
All inputs are finite; a program needn't handle non-finite values.
Results may differ from a plain program's by a relative error of at most 0.0017.
Values may be sent and summed in bfloat16 or wider, within the bound.
No kernel may reach another device: no remote copies, remote signals or barrier semaphores. Data moves between devices by JAX's collectives and lax.ppermute only.
A program may use at most 64 MiB of HBM per device.

v0:
```python
import jax
import jax.numpy as jnp
from jax import lax
from jax.sharding import PartitionSpec as P

STRIP = 128
NOV = 4
TILE = 512
KSIZE = 11
CELL = 128
NCELL = 16
PASSES = 3
CAUCHY = 2.0
OUTLIER = 3.0


def local_coadd(warped_all, var_all):
    values = warped_all.astype(jnp.float32)
    weights = var_all.astype(jnp.float32)
    root_weight = jnp.sqrt(weights)
    coadd_field = jnp.sum(weights * values, axis=0) / jnp.sum(weights, axis=0)
    for pass_index in range(PASSES):
        scaled = (values - coadd_field[None]) * root_weight / CAUCHY
        cauchy = weights / (1.0 + scaled * scaled)
        coadd_field = jnp.sum(cauchy * values, axis=0) / jnp.sum(cauchy, axis=0)
    return coadd_field


def psf_match(blotted, cell_grid, kernel_table):
    tile_side = blotted.shape[1]
    blocks = tile_side // CELL
    half_width = KSIZE // 2
    window = CELL + KSIZE - 1
    picker = (cell_grid.reshape(-1)[:, None] == jnp.arange(NCELL, dtype=jnp.int32)[None, :]).astype(
        jnp.bfloat16
    )
    tap_rows = jnp.dot(picker, kernel_table, preferred_element_type=jnp.float32)
    tap_rows = tap_rows.reshape(blocks, blocks, KSIZE, KSIZE)
    source = jnp.arange(window, dtype=jnp.int32)[:, None]
    target = jnp.arange(CELL, dtype=jnp.int32)[None, :]
    diagonal = (
        (source - target)[None] == jnp.arange(KSIZE, dtype=jnp.int32)[:, None, None]
    ).astype(jnp.float32)
    banded_all = jnp.einsum(
        "xyab,bcl->xyacl", tap_rows, diagonal, precision=lax.Precision.HIGHEST
    ).astype(jnp.bfloat16)
    padded = jnp.pad(blotted, ((half_width, half_width), (half_width, half_width)))
    row_parts = []
    for row_block in range(blocks):
        rows_window = lax.slice_in_dim(padded, row_block * CELL, row_block * CELL + window, axis=0)
        col_parts = []
        for col_block in range(blocks):
            cols_window = lax.slice_in_dim(
                rows_window, col_block * CELL, col_block * CELL + window, axis=1
            )
            horizontal = jnp.einsum(
                "rc,acl->arl",
                cols_window,
                banded_all[row_block, col_block],
                preferred_element_type=jnp.float32,
            )
            summed = horizontal[0, 0:CELL, :]
            for tap_row in range(1, KSIZE):
                summed = summed + horizontal[tap_row, tap_row : tap_row + CELL, :]
            col_parts.append(summed)
        row_parts.append(jnp.concatenate(col_parts, axis=1))
    return jnp.concatenate(row_parts, axis=0)


def shards(
    warped,
    inv_var,
    intersection,
    col_start,
    row_interp,
    col_interp,
    cell_ids,
    kernels,
    science,
    inv_sigma,
):
    warped_all, var_all = (
        lax.all_to_all(warped, "visit", split_axis=2, concat_axis=0, tiled=True),
        lax.all_to_all(inv_var, "visit", split_axis=2, concat_axis=0, tiled=True),
    )
    column_share = local_coadd(warped_all, var_all)
    coadd_field = lax.all_gather(column_share, "visit", axis=1, tiled=True)
    coadd_low = coadd_field.astype(jnp.bfloat16)
    strips = intersection[0, 0]
    start_col = col_start[0, 0]
    rows_map = row_interp[0, 0]
    shard_rows = lax.all_gather(coadd_low, "sky", axis=0, tiled=True)
    first_row = jnp.int32(0)
    row_count = shard_rows.shape[0]
    block_rows = min(row_count, STRIP)
    total = jnp.zeros((TILE, TILE), jnp.float32)
    for block_index in range(row_count // block_rows):
        block_first = first_row + block_index * block_rows
        strip_of = block_first // STRIP
        inside = block_first % STRIP
        matches = strips == strip_of
        slot_index = jnp.sum(jnp.where(matches, jnp.arange(NOV, dtype=jnp.int32), 0))
        present = jnp.any(matches)
        block_data = shard_rows[block_index * block_rows : (block_index + 1) * block_rows]

        def add_block(current):
            chosen = lax.dynamic_slice_in_dim(rows_map, slot_index * STRIP + inside, block_rows, 1)
            columns = lax.dynamic_slice_in_dim(block_data, start_col, TILE, 1)
            return current + jnp.dot(chosen, columns, preferred_element_type=jnp.float32)

        total = lax.cond(present, add_block, lambda current: current, total)
    blotted = jnp.dot(
        total.astype(jnp.bfloat16), col_interp[0, 0], preferred_element_type=jnp.float32
    ).astype(jnp.bfloat16)
    matched = psf_match(blotted, cell_ids[0, 0], kernels[0, 0])
    residual = (
        (science[0, 0].astype(jnp.float32) - matched)
        * inv_sigma[0, 0].astype(jnp.float32)
        / OUTLIER
    )
    outlier = 1.0 / (1.0 + residual * residual)
    return (coadd_field, outlier[None, None])


def solution(mesh):
    in_specs = (
        P("visit", "sky", None),
        P("visit", "sky", None),
        P("visit", "sky", None),
        P("visit", "sky"),
        P("visit", "sky", None, None),
        P("visit", "sky", None, None),
        P("visit", "sky", None, None),
        P("visit", "sky", None, None),
        P("visit", "sky", None, None),
        P("visit", "sky", None, None),
    )
    out_specs = (P("sky", None), P("visit", "sky", None, None))
    return jax.shard_map(shards, mesh=mesh, in_specs=in_specs, out_specs=out_specs, check_vma=False)
```

profile of v0, /device:TPU:0, one launch (start us, length us, event | category | flops | bytes accessed | tf_op | source)
XLA Modules:
  0.0 203.1 jit_solution(12061333700261532114)
XLA Ops:
  7.2 3.8 %copy.119 = bf16[2,128,2048]{1,0,2:T(2,128)(2,1)} copy(bf16[2,128,2048]{2,1,0:T(8,128)(2,1)} %param.18) | data formatting | bytes 2097152 | tf_op args[0]
  11.0 7.3 %all-to-all-start.1 = ((bf16[2,128,2048]{1,0,2:T(2,128)(2,1)}), bf16[2,128,2048]{1,0,2:T(2,128)(2,1)S(1)}, u32[]{:S(2)}, u32[]{:S(2)}) async-start(bf16[2,128,2048]{1,0,2:T(2,128)(2,1)} %copy.119), calls=%async_computation.1 | async-start | bytes 2097152 | tf_op jit(solution)/shard_map/all_to_all | solution.py:83
  18.3 2.0 copy.116
  20.3 23.8 %all-to-all-done.1 = bf16[2,128,2048]{1,0,2:T(2,128)(2,1)S(1)} async-done(((bf16[2,128,2048]{1,0,2:T(2,128)(2,1)}), bf16[2,128,2048]{1,0,2:T(2,128)(2,1)S(1)}, u32[]{:S(2)}, u32[]{:S(2)}) %all-to-all-start.1) | async-done | bytes 1048608 | tf_op jit(solution)/shard_map/all_to_all | solution.py:83
  44.0 4.2 %all-to-all-start = ((bf16[2,128,2048]{1,0,2:T(2,128)(2,1)}), bf16[2,128,2048]{1,0,2:T(2,128)(2,1)}, u32[]{:S(2)}, u32[]{:S(2)}) async-start(bf16[2,128,2048]{1,0,2:T(2,128)(2,1)} %copy.116), calls=%async_computation | async-start | bytes 2097152 | tf_op jit(solution)/shard_map/all_to_all | solution.py:84
  48.3 1.1 copy.120
  49.4 1.5 copy.121
  50.9 22.9 %all-to-all-done = bf16[2,128,2048]{1,0,2:T(2,128)(2,1)} async-done(((bf16[2,128,2048]{1,0,2:T(2,128)(2,1)}), bf16[2,128,2048]{1,0,2:T(2,128)(2,1)}, u32[]{:S(2)}, u32[]{:S(2)}) %all-to-all-start) | async-done | bytes 1048608 | tf_op jit(solution)/shard_map/all_to_all | solution.py:84
  73.8 2.3 %copy.117 = bf16[2,128,2048]{1,2,0:T(8,128)(2,1)} copy(bf16[2,128,2048]{1,0,2:T(2,128)(2,1)} %all-to-all-done) | data formatting | bytes 2097152 | tf_op jit(solution)/shard_map/all_to_all | solution.py:84
  76.2 2.6 %copy.118 = f32[2,128,8,256]{3,1,0,2:T(8,128)} copy(bf16[2,128,8,256]{1,3,2,0:T(8,128)(2,1)} %bitcast.283) | data formatting | bytes 3145728 | tf_op jit(solution)/shard_map/convert_element_type | solution.py:19
  78.8 2.0 %bitcast_reduce_fusion = (f32[128,256]{1,0:T(8,128)S(1)}, f32[128,256]{1,0:T(8,128)S(1)}) fusion(f32[2,128,8,256]{3,1,0,2:T(8,128)} %copy.118, f32[2,128,8,256]{3,1,0,2:T(8,128)S(1)} %copy.121), kind=kLoop, calls=%fused_computation.52 | loop fusion | flops 1507328 | bytes 4456448 | tf_op jit(solution)/shard_map/reduce_sum | solution.py:21
  81.0 1.2 fusion.106
  82.2 1.2 fusion.105
  83.5 1.2 fusion.104
  85.0 0.7 div.72
  85.7 39.2 %all-gather.3.cloned.1.call-done = f32[128,2048]{0,1:T(8,128)} async-done(((f32[128,256]{0,1:T(8,128)}), f32[128,2048]{0,1:T(8,128)}) %all-gather.3.cloned.1.call-update) | async-done | bytes 1048592 | tf_op jit(solution)/shard_map/all_gather | solution.py:87
  124.9 2.1 %convert_element_type.88 = bf16[128,2048]{0,1:T(8,128)(2,1)} convert(f32[128,2048]{0,1:T(8,128)} %all-gather.3.cloned.1.call-done) | non-fusion elementwise | flops 262144 | bytes 1572864 | tf_op jit(solution)/shard_map/convert_element_type | solution.py:88
  127.0 0.7 fusion.125
  130.9 7.5 %convolution_convert_fusion = bf16[4,4,11,138,128]{4,2,3,1,0:T(8,128)(2,1)S(1)} fusion(s32[138,128]{1,0:T(8,128)S(1)} %iota_subtract_fusion, f32[4,4,11,11,1]{3,1,2,0,4:T(4,128)S(1)} %convolution_bitcast_fusion.16), kind=kOutput, calls=%fused_computation.24 | convolution fusion | flops 413673216 | bytes 6296128 | tf_op jit(solution)/shard_map/xyab,bcl->xyacl/dot_general | solution.py:44
  138.4 3.4 %slice_bitcast_fusion.15 = (bf16[11,138,128]{2,0,1:T(8,128)(2,1)}, bf16[11,138,128]{2,0,1:T(8,128)(2,1)}, bf16[11,138,128]{2,0,1:T(8,128)(2,1)}, bf16[11,138,128...) fusion(bf16[4,4,11,138,128]{4,2,3,1,0:T(8,128)(2,1)S(1)} %convo, ...), kind=kLoop, calls=%fused_computation.106 | loop fusion | bytes 12435456 | tf_op jit(solution)/shard_map/squeeze | solution.py:59
  141.8 1.3 copy.146
  143.1 5.7 %all-gather.5.cloned.1.call-done = bf16[512,2048]{0,1:T(8,128)(2,1)} async-done(((bf16[128,2048]{0,1:T(8,128)(2,1)}), bf16[512,2048]{0,1:T(8,128)(2,1)}) %all-gather.5.cloned.1.call-update) | async-done | bytes 2097168 | tf_op jit(solution)/shard_map/all_gather | solution.py:92
  148.7 7.5 %conditional.4 = (f32[512,512]{1,0:T(8,128)S(1)}) conditional(s32[]{:T(128)} %convert_element_type.87, () %tuple.44, (pred[1,1,4]{2,1,0:T(4,128)(4,1)S(1)}, bf16[512,512]{1,0:T(8,128)(2,1)}, s32[]{:T(128)}, bf16[512,2048]{0,1:T(8,128)(2,1)}, s32[]{:T(128)}, /*index=5*/s32[4]{0:T(128)S(1)}, s32[4]{0:T(128)S(1)}) %tuple.105), branch_computations={%region_13.14_spmd, %region_14.15_spmd} | conditional | flops 67108880 | bytes 6553740 | solution.py:111
  150.7 0.7 fusion.3
  152.0 2.9 %copy.126 = bf16[512,2048]{1,0:T(8,128)(2,1)S(1)} copy(bf16[512,2048]{0,1:T(8,128)(2,1)} %get-tuple-element.197) | data formatting | bytes 4194304 | tf_op jit(solution)/shard_map
  155.0 1.3 fusion
  156.3 9.5 %conditional.5 = (f32[512,512]{1,0:T(8,128)S(1)}) conditional(s32[]{:T(128)} %convert_element_type.86, f32[512,512]{1,0:T(8,128)S(1)} %get-tuple-element.261, (pred[1,1,4]{2,1,0:T(4,128)(4,1)S(1)}, bf16[512,512]{1,0:T(8,128)(2,1)}, s32[]{:T(128)}, bf16[512,2048]{0,1:T(8,128)(2,1)}, f32[512,512]{1,0:T(8,128)S(1)}, /*index=5*/s32[]{:T(128)}, ...), branch_computations={%region_16.17_spmd, %region_17.18_spmd} | conditional | flops 67371024 | bytes 7602316 | solution.py:111
  158.2 0.6 fusion.7
  159.4 4.0 %copy.127 = bf16[512,2048]{1,0:T(8,128)(2,1)} copy(bf16[512,2048]{0,1:T(8,128)(2,1)} %get-tuple-element.204) | data formatting | bytes 4194304 | tf_op jit(solution)/shard_map
  163.4 1.1 slice.877
  164.5 1.3 convolution_add_fusion
  165.8 9.6 %conditional.6 = (f32[512,512]{1,0:T(8,128)S(1)}) conditional(s32[]{:T(128)} %convert_element_type.85, f32[512,512]{1,0:T(8,128)S(1)} %get-tuple-element.262, (pred[1,1,4]{2,1,0:T(4,128)(4,1)S(1)}, bf16[512,512]{1,0:T(8,128)(2,1)}, s32[]{:T(128)}, bf16[512,2048]{0,1:T(8,128)(2,1)}, f32[512,512]{1,0:T(8,128)S(1)}, /*index=5*/s32[]{:T(128)}, ...), branch_computations={%region_19.20_spmd, %region_20.21_spmd} | conditional | flops 67371024 | bytes 7602316 | solution.py:111
  167.9 0.6 fusion.11
  169.1 4.0 %copy.128 = bf16[512,2048]{1,0:T(8,128)(2,1)} copy(bf16[512,2048]{0,1:T(8,128)(2,1)} %get-tuple-element.212) | data formatting | bytes 4194304 | tf_op jit(solution)/shard_map
  173.0 1.1 slice.878
  174.1 1.3 convolution_add_fusion.1
  175.4 9.4 %conditional.7 = (f32[512,512]{1,0:T(8,128)S(1)}) conditional(s32[]{:T(128)} %convert_element_type.84, f32[512,512]{1,0:T(8,128)S(1)} %get-tuple-element.263, (pred[1,1,4]{2,1,0:T(4,128)(4,1)S(1)}, s32[4]{0:T(128)S(1)}, bf16[512,512]{1,0:T(8,128)(2,1)}, bf16[512,2048]{0,1:T(8,128)(2,1)}, s32[]{:T(128)}, /*index=5*/f32[512,512]{1,0:T(8,128)S(1)}) %tuple.108), branch_computations={%region_21.22_spmd, %region_22.24_spmd} | conditional | flops 67371024 | bytes 7602296 | solution.py:111
  177.4 0.6 fusion.15
  178.5 4.0 %copy.129 = bf16[512,2048]{1,0:T(8,128)(2,1)} copy(bf16[512,2048]{0,1:T(8,128)(2,1)} %get-tuple-element.220) | data formatting | bytes 4194304 | tf_op jit(solution)/shard_map
  182.5 1.1 slice.879
  183.6 1.3 convolution_add_fusion.2
  184.9 0.4 convolution_convert_fusion.1
  185.3 0.6 copy-done.17
  188.5 0.3 convolution_bitcast_fusion.4
  192.3 0.3 convolution_bitcast_fusion.11
  193.8 0.3 convolution_bitcast_fusion.14
  194.3 0.5 copy-done.19
  195.0 1.3 fusion.42
  (96 shorter events, 8.4 us)
Async XLA Ops:
  7.2 177.7 %copy-start = (bf16[1,1,512,512]{3,2,1,0:T(8,128)(2,1)S(1)}, bf16[1,1,512,512]{3,2,1,0:T(8,128)(2,1)}, u32[]{:S(2)}) copy-start(bf16[1,1,512,512]{3,2,1,0:T(8,128)(2,1)} %param.23) | copy-start | bytes 1572868
  7.2 11.1 %copy-start.18 = (bf16[2,128,2048]{2,1,0:T(8,128)(2,1)S(1)}, bf16[2,128,2048]{2,1,0:T(8,128)(2,1)}, u32[]{:S(2)}) copy-start(bf16[2,128,2048]{2,1,0:T(8,128)(2,1)} %param.19) | copy-start | bytes 3145732
  11.0 33.0 %all-to-all-start.1 = ((bf16[2,128,2048]{1,0,2:T(2,128)(2,1)}), bf16[2,128,2048]{1,0,2:T(2,128)(2,1)S(1)}, u32[]{:S(2)}, u32[]{:S(2)}) async-start(bf16[2,128,2048]{1,0,2:T(2,128)(2,1)} %copy.119), calls=%async_computation.1 | async-start | bytes 2097152 | tf_op jit(solution)/shard_map/all_to_all | solution.py:83
  44.0 29.8 %all-to-all-start = ((bf16[2,128,2048]{1,0,2:T(2,128)(2,1)}), bf16[2,128,2048]{1,0,2:T(2,128)(2,1)}, u32[]{:S(2)}, u32[]{:S(2)}) async-start(bf16[2,128,2048]{1,0,2:T(2,128)(2,1)} %copy.116), calls=%async_computation | async-start | bytes 2097152 | tf_op jit(solution)/shard_map/all_to_all | solution.py:84
  48.3 76.7 %all-gather.3.cloned.1.call-start = ((), (), s32[]{:S(2)}) async-start(), calls=%async_computation.2 | async-start | bytes 1179648 | tf_op jit(solution)/shard_map/all_gather | solution.py:87
  78.8 2.2 %copy-start.1 = (f32[2,128,8,256]{3,1,0,2:T(8,128)S(1)}, f32[2,128,8,256]{3,1,0,2:T(8,128)}, u32[]{:S(2)}) copy-start(f32[2,128,8,256]{3,1,0,2:T(8,128)} %copy.118) | copy-start | bytes 6291460
  84.7 42.3 %copy-start.23 = (s32[1,1,4]{2,1,0:T(1,128)S(1)}, s32[1,1,4]{2,1,0:T(1,128)}, u32[]{:S(2)}) copy-start(s32[1,1,4]{2,1,0:T(1,128)} %param.20) | copy-start | bytes 52
  84.7 45.6 %copy-start.21 = (bf16[1,1,16,121]{3,2,1,0:T(8,128)(2,1)S(1)}, bf16[1,1,16,121]{3,2,1,0:T(8,128)(2,1)}, u32[]{:S(2)}) copy-start(bf16[1,1,16,121]{3,2,1,0:T(8,128)(2,1)} %param.25) | copy-start | bytes 11620
  84.7 45.9 %copy-start.22 = (s32[1,1,4,4]{3,2,1,0:T(4,128)S(1)}, s32[1,1,4,4]{3,2,1,0:T(4,128)}, u32[]{:S(2)}) copy-start(s32[1,1,4,4]{3,2,1,0:T(4,128)} %param.24) | copy-start | bytes 196
  85.7 63.1 %all-gather.5.cloned.1.call-start = ((), (), s32[]{:S(2)}) async-start(), calls=%async_computation.3 | async-start | bytes 2621440 | tf_op jit(solution)/shard_map/all_gather | solution.py:92
  138.4 3.4 %copy-start.2 = (f32[128,2048]{0,1:T(8,128)S(1)}, f32[128,2048]{0,1:T(8,128)}, u32[]{:S(2)}) copy-start(f32[128,2048]{0,1:T(8,128)} %all-gather.3.cloned.1.call-done) | copy-start | bytes 3145732
  184.9 1.1 copy-start.17
  184.9 1.4 copy-start.16
  185.9 1.1 copy-start.15
  186.3 1.1 copy-start.14
  187.0 1.1 copy-start.13
  187.4 1.1 copy-start.12
  188.1 1.1 copy-start.11
  188.5 1.1 copy-start.10
  189.0 1.1 copy-start.9
  189.6 1.1 copy-start.8
  190.1 1.1 copy-start.7
  190.7 1.1 copy-start.6
  191.1 1.1 copy-start.5
  191.8 1.1 copy-start.4
  192.3 1.1 copy-start.3
  193.8 1.0 copy-start.19
  193.8 1.2 copy-start.20
Sparse Core Ops, SparseCore 0:
  85.8 39.1 all-gather.2
  127.2 21.5 all-gather.4
where the time goes:
time: 204 us; the launch traced here: 203 us
  waiting for transfers between devices  91.6 us (45%)
  local copies, waits for them, and re-layouts  39.7 us (19%)
  matrix products  18.5 us (9%)
  between operations  17.1 us (8%)
  other arithmetic  14.2 us (7%)
  starting transfers between devices  11.6 us (6%)
  loops' own time  10.3 us (5%)
    all_gather x1, waiting for transfers between devices, shards(): coadd_field = lax.all_gather(column_share, 'visit', axis=1, tiled=True)  39.2 us
    all_to_all x1, waiting for transfers between devices, shards(): lax.all_to_all(warped, 'visit', split_axis=2, concat_axis=0, tiled=True)  23.8 us
    all_to_all x1, waiting for transfers between devices, shards(): lax.all_to_all(inv_var, 'visit', split_axis=2, concat_axis=0, tiled=True)  22.9 us
    another operation x4, local copies, waits for them, and re-layouts  14.8 us
    unnamed x53, local copies, waits for them, and re-layouts  10.5 us
    another operation x4, loops' own time, shards(): total = lax.cond(present, add_block, lambda current: current, total)  10.3 us
    dot_general x1, matrix products, psf_match(): jnp.einsum('xyab,bcl->xyacl', tap_rows, diagonal, precision=lax.Precision...  7.51 us
    all_to_all x1, starting transfers between devices, shards(): lax.all_to_all(warped, 'visit', split_axis=2, concat_axis=0, tiled=True)  7.28 us
  transfers between devices with their start and end apart: 4, of which 4 were waited for; matrix products, arithmetic and copies ran while one was open for 9% of the time, Pallas kernels for 0%

commit v1 on v0

--- a/solution.py
+++ b/solution.py
@@ -12,6 +12,29 @@
 PASSES = 3
 CAUCHY = 2.0
 OUTLIER = 3.0
+
+
+def in_blocks(shard, dim, size):
+    shape = shard.shape
+    blocks = shard.reshape(*shape[:dim], size, shape[dim] // size, *shape[dim + 1 :])
+    return jnp.moveaxis(blocks, dim, 0)
+
+
+def joined_along(tiles, dim):
+    tiles = jnp.moveaxis(tiles, 0, dim)
+    dims = tiles.shape
+    return tiles.reshape(*dims[:dim], dims[dim] * dims[dim + 1], *dims[dim + 2 :])
+
+
+def swapped_with_each(x, axis, split_dim, concat_dim):
+    size, index = (lax.axis_size(axis), lax.axis_index(axis))
+    parts = in_blocks(x, split_dim, size)
+    outs = [parts[index]]
+    for turn in range(1, size):
+        sent = parts[index ^ turn]
+        outs.append(lax.ppermute(sent, axis, [(i, i ^ turn) for i in range(size)]))
+    parts = jnp.stack(outs)[index ^ jnp.arange(size)]
+    return joined_along(parts, concat_dim)
 
 
 def local_coadd(warped_all, var_all):
@@ -81,7 +104,7 @@
 ):
     warped_all, var_all = (
         lax.all_to_all(warped, "visit", split_axis=2, concat_axis=0, tiled=True),
-        lax.all_to_all(inv_var, "visit", split_axis=2, concat_axis=0, tiled=True),
+        swapped_with_each(inv_var, "visit", 2, 0),
     )
     column_share = local_coadd(warped_all, var_all)
     coadd_field = lax.all_gather(column_share, "visit", axis=1, tiled=True)

time: 204 us -> 182 us (0.89)
  waiting for transfers between devices: 91.6 us -> 64.9 us
  starting transfers between devices: 11.6 us -> 25.6 us
  local copies, waits for them, and re-layouts: 39.7 us -> 29.2 us
    all_to_all x1, waiting for transfers between devices: 23.8 us -> 0.01 us  [shards(): lax.all_to_all(warped, 'visit', split_axis=2, concat_axis=0, tiled=True)]
    all_to_all x1 -> x0, waiting for transfers between devices: 22.9 us -> none  [shards(): lax.all_to_all(inv_var, 'visit', split_axis=2, concat_axis=0, tiled=True)]
    ppermute x0 -> x7, starting transfers between devices: none -> 18.2 us  [swapped_with_each(): outs.append(lax.ppermute(sent, axis, [(i, i ^ turn) for i in range(size)]))]
    ppermute x0 -> x7, waiting for transfers between devices: none -> 16.2 us  [swapped_with_each(): outs.append(lax.ppermute(sent, axis, [(i, i ^ turn) for i in range(size)]))]
    another operation x4 -> x10, local copies, waits for them, and re-layouts: 14.8 us -> 4.53 us
    all_to_all x1 -> x0, starting transfers between devices: 4.24 us -> none  [shards(): lax.all_to_all(inv_var, 'visit', split_axis=2, concat_axis=0, tiled=True)]
    convert_element_type x1 -> x0, local copies, waits for them, and re-layouts: 2.59 us -> none  [local_coadd(): weights = var_all.astype(jnp.float32)]
    all_to_all x1 -> x0, local copies, waits for them, and re-layouts: 2.33 us -> none  [shards(): lax.all_to_all(inv_var, 'visit', split_axis=2, concat_axis=0, tiled=True)]
  transfers between devices with their start and end apart: 4 -> 10, of which waited for: 4 -> 5; matrix products, arithmetic and copies ran while one was open for 9% -> 13% of each run, Pallas kernels for 0% -> 0%
where the time goes in v1:
time: 182 us; the launch traced here: 181 us
  waiting for transfers between devices  64.9 us (36%)
  local copies, waits for them, and re-layouts  29.2 us (16%)
  starting transfers between devices  25.6 us (14%)
  matrix products  18.5 us (10%)
  between operations  17.2 us (9%)
  other arithmetic  14.3 us (8%)
  loops' own time  10.8 us (6%)
    all_gather x1, waiting for transfers between devices, shards(): coadd_field = lax.all_gather(column_share, 'visit', axis=1, tiled=True)  41.4 us
    ppermute x7, starting transfers between devices, swapped_with_each(): outs.append(lax.ppermute(sent, axis, [(i, i ^ turn) for i in range(size)]))  18.2 us
    ppermute x7, waiting for transfers between devices, swapped_with_each(): outs.append(lax.ppermute(sent, axis, [(i, i ^ turn) for i in range(size)]))  16.2 us
    unnamed x52, local copies, waits for them, and re-layouts  12.8 us
    another operation x4, loops' own time, shards(): total = lax.cond(present, add_block, lambda current: current, total)  10.8 us
    dot_general x1, matrix products, psf_match(): jnp.einsum('xyab,bcl->xyacl', tap_rows, diagonal, precision=lax.Precision...  7.48 us
    all_to_all x1, starting transfers between devices, shards(): lax.all_to_all(warped, 'visit', split_axis=2, concat_axis=0, tiled=True)  7.28 us
    all_gather x1, waiting for transfers between devices, shards(): shard_rows = lax.all_gather(coadd_low, 'sky', axis=0, tiled=True)  7.24 us
  transfers between devices with their start and end apart: 10, of which 5 were waited for; matrix products, arithmetic and copies ran while one was open for 13% of the time, Pallas kernels for 0%

profile of v1, /device:TPU:0, one launch (start us, length us, event | category | flops | bytes accessed | tf_op | source)
XLA Modules:
  0.0 180.5 jit_solution(9944696654322616430)
XLA Ops:
  7.2 3.7 %copy.82 = bf16[2,128,2048]{1,0,2:T(2,128)(2,1)} copy(bf16[2,128,2048]{2,1,0:T(8,128)(2,1)} %param.18) | data formatting | bytes 2097152 | tf_op args[0]
  10.9 7.3 %all-to-all-start = ((bf16[2,128,2048]{1,0,2:T(2,128)(2,1)}), bf16[2,128,2048]{1,0,2:T(2,128)(2,1)S(1)}, u32[]{:S(2)}, u32[]{:S(2)}) async-start(bf16[2,128,2048]{1,0,2:T(2,128)(2,1)} %copy.82), calls=%async_computation | async-start | bytes 2097152 | tf_op jit(solution)/shard_map/all_to_all | solution.py:106
  18.3 1.6 copy.73
  19.9 0.8 constant_dynamic-slice_fusion
  20.7 1.7 copy.75
  22.3 1.9 %collective-permute-start = (bf16[2,128,256]{2,1,0:T(8,128)(2,1)}, bf16[2,128,256]{2,1,0:T(8,128)(2,1)}, u32[]{:S(2)}, u32[]{:S(2)}) collective-permute-start(bf16[2,128,256]{2,1,0:T(8,128)(2,1)} %bitcast.6), channel_id=1, source_target_pairs={{0,4},{4,0},{8,12},{12,8},{16,20},{20,16},{24,28},{28,24},{1,5},{5... | collective-permute-start | bytes 393224 | tf_op jit(solution)/shard_map/ppermute | solution.py:35
  24.3 0.8 copy.76
  25.1 1.5 collective-permute-start.1
  26.5 0.8 copy.77
  27.5 2.9 %collective-permute-start.3 = (bf16[2,128,256]{2,1,0:T(8,128)(2,1)S(1)}, bf16[2,128,256]{2,1,0:T(8,128)(2,1)}, u32[]{:S(2)}, u32[]{:S(2)}) collective-permute-start(bf16[2,128,256]{2,1,0:T(8,128)(2,1)S(1)} %bitcast.263), channel_id=1, source_target_pairs={{0,16},{4,20},{8,24},{12,28},{16,0},{20,4},{24,8},{28,12},{1,17},{... | collective-permute-start | bytes 393224 | tf_op jit(solution)/shard_map/ppermute | solution.py:35
  30.5 1.5 collective-permute-start.4
  32.5 5.7 %collective-permute-start.5 = (bf16[2,128,256]{2,1,0:T(8,128)(2,1)S(1)}, bf16[2,128,256]{2,1,0:T(8,128)(2,1)S(1)}, u32[]{:S(2)}, u32[]{:S(2)}) collective-permute-start(bf16[2,128,256]{2,1,0:T(8,128)(2,1)S(1)} %bitcast.264), channel_id=1, source_target_pairs={{0,24},{4,28},{8,16},{12,20},{16,8},{20,12},{24,0},{28,4},{1,25},{... | collective-permute-start | bytes 393224 | tf_op jit(solution)/shard_map/ppermute | solution.py:35
  38.2 0.9 bitcast_dynamic-update-slice_fusion.6
  39.4 4.6 %collective-permute-start.6 = (bf16[2,128,256]{2,1,0:T(8,128)(2,1)S(1)}, bf16[2,128,256]{2,1,0:T(8,128)(2,1)S(1)}, u32[]{:S(2)}, u32[]{:S(2)}) collective-permute-start(bf16[2,128,256]{2,1,0:T(8,128)(2,1)S(1)} %bitcast.261), channel_id=1, source_target_pairs={{0,28},{4,24},{8,20},{12,16},{16,12},{20,8},{24,4},{28,0},{1,29},{... | collective-permute-start | bytes 393224 | tf_op jit(solution)/shard_map/ppermute | solution.py:35
  44.0 0.9 bitcast_dynamic-update-slice_fusion.5
  44.9 0.9 bitcast_dynamic-update-slice_fusion.4
  45.8 13.7 %collective-permute-done.3 = bf16[2,128,256]{2,1,0:T(8,128)(2,1)} collective-permute-done((bf16[2,128,256]{2,1,0:T(8,128)(2,1)S(1)}, bf16[2,128,256]{2,1,0:T(8,128)(2,1)}, u32[]{:S(2)}, u32[]{:S(2)}) %collective-permute-start.3) | collective-permute-done | bytes 131104 | tf_op jit(solution)/shard_map/ppermute | solution.py:35
  59.5 0.9 bitcast_dynamic-update-slice_fusion.3
  60.4 2.3 %collective-permute-done.4 = bf16[2,128,256]{2,1,0:T(8,128)(2,1)S(1)} collective-permute-done((bf16[2,128,256]{2,1,0:T(8,128)(2,1)S(1)}, bf16[2,128,256]{2,1,0:T(8,128)(2,1)S(1)}, u32[]{:S(2)}, u32[]{:S(2)}) %collective-permute-start.4) | collective-permute-done | bytes 131104 | tf_op jit(solution)/shard_map/ppermute | solution.py:35
  62.7 1.6 gather_fusion
  64.3 1.1 copy.83
  65.4 1.5 copy.84
  66.9 1.6 convert_reduce_fusion
  68.6 1.3 fusion.40
  69.9 1.3 fusion.41
  71.2 1.3 fusion.42
  73.3 41.4 %all-gather.3.cloned.1.call-done = f32[128,2048]{1,0:T(8,128)} async-done(((f32[128,256]{1,0:T(8,128)}), f32[128,2048]{1,0:T(8,128)}) %all-gather.3.cloned.1.call-update) | async-done | bytes 1048592 | tf_op jit(solution)/shard_map/all_gather | solution.py:110
  114.7 2.1 %convert_element_type.80 = bf16[128,2048]{1,0:T(8,128)(2,1)} convert(f32[128,2048]{1,0:T(8,128)} %all-gather.3.cloned.1.call-done) | non-fusion elementwise | flops 262144 | bytes 1572864 | tf_op jit(solution)/shard_map/convert_element_type | solution.py:111
  116.8 0.7 fusion.123
  120.6 7.5 %convolution_convert_fusion = bf16[4,4,11,138,128]{4,2,3,1,0:T(8,128)(2,1)S(1)} fusion(s32[138,128]{1,0:T(8,128)S(1)} %iota_subtract_fusion, f32[4,4,11,11,1]{3,1,2,0,4:T(4,128)S(1)} %convolution_bitcast_fusion.16), kind=kOutput, calls=%fused_computation.25 | convolution fusion | flops 413673216 | bytes 6296128 | tf_op jit(solution)/shard_map/xyab,bcl->xyacl/dot_general | solution.py:67
  128.1 3.1 %slice_bitcast_fusion.15 = (bf16[11,138,128]{2,0,1:T(8,128)(2,1)}, bf16[11,138,128]{2,0,1:T(8,128)(2,1)}, bf16[11,138,128]{2,0,1:T(8,128)(2,1)}, bf16[11,138,128...) fusion(bf16[4,4,11,138,128]{4,2,3,1,0:T(8,128)(2,1)S(1)} %convo, ...), kind=kLoop, calls=%fused_computation.110 | loop fusion | bytes 12435456 | tf_op jit(solution)/shard_map/squeeze | solution.py:82
  131.3 7.2 %all-gather.5.cloned.1.call-done = bf16[512,2048]{1,0:T(8,128)(2,1)} async-done(((bf16[128,2048]{1,0:T(8,128)(2,1)}), bf16[512,2048]{1,0:T(8,128)(2,1)}) %all-gather.5.cloned.1.call-update) | async-done | bytes 2097168 | tf_op jit(solution)/shard_map/all_gather | solution.py:115
  138.5 5.7 %conditional.4 = (f32[512,512]{1,0:T(8,128)S(1)}) conditional(s32[]{:T(128)} %convert_element_type.79, () %tuple.44, (pred[1,1,4]{2,1,0:T(4,128)(4,1)S(1)}, bf16[512,512]{1,0:T(8,128)(2,1)}, s32[]{:T(128)}, bf16[512,2048]{1,0:T(8,128)(2,1)}, s32[]{:T(128)}, /*index=5*/s32[4]{0:T(128)S(1)}, s32[4]{0:T(128)S(1)}) %tuple.99), branch_computations={%region_13.14_spmd, %region_14.15_spmd} | conditional | flops 67108880 | bytes 2359436 | solution.py:134
  140.5 0.7 fusion.3
  141.9 1.1 slice.873
  142.9 1.3 fusion
  144.2 5.7 %conditional.5 = (f32[512,512]{1,0:T(8,128)S(1)}) conditional(s32[]{:T(128)} %convert_element_type.78, f32[512,512]{1,0:T(8,128)S(1)} %get-tuple-element.180, (pred[1,1,4]{2,1,0:T(4,128)(4,1)S(1)}, bf16[512,512]{1,0:T(8,128)(2,1)}, s32[]{:T(128)}, bf16[512,2048]{1,0:T(8,128)(2,1)}, f32[512,512]{1,0:T(8,128)S(1)}, /*index=5*/s32[]{:T(128)}, ...), branch_computations={%region_16.17_spmd, %region_17.18_spmd} | conditional | flops 67371024 | bytes 3408012 | solution.py:134
  146.2 0.7 fusion.7
  147.6 1.1 slice.874
  148.7 1.3 convolution_add_fusion
  150.0 5.9 %conditional.6 = (f32[512,512]{1,0:T(8,128)S(1)}) conditional(s32[]{:T(128)} %convert_element_type.77, f32[512,512]{1,0:T(8,128)S(1)} %get-tuple-element.181, (pred[1,1,4]{2,1,0:T(4,128)(4,1)S(1)}, bf16[512,512]{1,0:T(8,128)(2,1)}, s32[]{:T(128)}, bf16[512,2048]{1,0:T(8,128)(2,1)}, f32[512,512]{1,0:T(8,128)S(1)}, /*index=5*/s32[]{:T(128)}, ...), branch_computations={%region_19.20_spmd, %region_20.21_spmd} | conditional | flops 67371024 | bytes 3408012 | solution.py:134
  153.5 1.1 slice.875
  154.6 1.3 convolution_add_fusion.1
  155.9 5.7 %conditional.7 = (f32[512,512]{1,0:T(8,128)S(1)}) conditional(s32[]{:T(128)} %convert_element_type.76, f32[512,512]{1,0:T(8,128)S(1)} %get-tuple-element.182, (pred[1,1,4]{2,1,0:T(4,128)(4,1)S(1)}, s32[4]{0:T(128)S(1)}, bf16[512,512]{1,0:T(8,128)(2,1)}, bf16[512,2048]{1,0:T(8,128)(2,1)}, s32[]{:T(128)}, /*index=5*/f32[512,512]{1,0:T(8,128)S(1)}) %tuple.102), branch_computations={%region_21.22_spmd, %region_22.24_spmd} | conditional | flops 67371024 | bytes 3407992 | solution.py:134
  159.3 1.1 slice.450
  160.4 1.3 convolution_add_fusion.2
  171.5 1.3 fusion.39
  172.7 1.0 copy.158
  (114 shorter events, 13.4 us)
Async XLA Ops:
  7.2 154.5 %copy-start = (bf16[1,1,512,512]{3,2,1,0:T(8,128)(2,1)S(1)}, bf16[1,1,512,512]{3,2,1,0:T(8,128)(2,1)}, u32[]{:S(2)}) copy-start(bf16[1,1,512,512]{3,2,1,0:T(8,128)(2,1)} %param.23) | copy-start | bytes 1572868
  10.9 53.4 %all-to-all-start = ((bf16[2,128,2048]{1,0,2:T(2,128)(2,1)}), bf16[2,128,2048]{1,0,2:T(2,128)(2,1)S(1)}, u32[]{:S(2)}, u32[]{:S(2)}) async-start(bf16[2,128,2048]{1,0,2:T(2,128)(2,1)} %copy.82), calls=%async_computation | async-start | bytes 2097152 | tf_op jit(solution)/shard_map/all_to_all | solution.py:106
  18.2 96.5 %all-gather.3.cloned.1.call-start = ((), (), s32[]{:S(2)}) async-start(), calls=%async_computation.1 | async-start | bytes 1179648 | tf_op jit(solution)/shard_map/all_gather | solution.py:110
  22.3 10.1 %collective-permute-start = (bf16[2,128,256]{2,1,0:T(8,128)(2,1)}, bf16[2,128,256]{2,1,0:T(8,128)(2,1)}, u32[]{:S(2)}, u32[]{:S(2)}) collective-permute-start(bf16[2,128,256]{2,1,0:T(8,128)(2,1)} %bitcast.6), channel_id=1, source_target_pairs={{0,4},{4,0},{8,12},{12,8},{16,20},{20,16},{24,28},{28,24},{1,5},{5... | collective-permute-start | bytes 393224 | tf_op jit(solution)/shard_map/ppermute | solution.py:35
  25.1 14.3 %collective-permute-start.1 = (bf16[2,128,256]{2,1,0:T(8,128)(2,1)}, bf16[2,128,256]{2,1,0:T(8,128)(2,1)}, u32[]{:S(2)}, u32[]{:S(2)}) collective-permute-start(bf16[2,128,256]{2,1,0:T(8,128)(2,1)} %bitcast.8), channel_id=1, source_target_pairs={{0,8},{4,12},{8,0},{12,4},{16,24},{20,28},{24,16},{28,20},{1,9},{5... | collective-permute-start | bytes 393224 | tf_op jit(solution)/shard_map/ppermute | solution.py:35
  27.3 17.6 %collective-permute-start.2 = (bf16[2,128,256]{2,1,0:T(8,128)(2,1)}, bf16[2,128,256]{2,1,0:T(8,128)(2,1)}, u32[]{:S(2)}, u32[]{:S(2)}) collective-permute-start(bf16[2,128,256]{2,1,0:T(8,128)(2,1)} %bitcast.10), channel_id=1, source_target_pairs={{0,12},{4,8},{8,4},{12,0},{16,28},{20,24},{24,20},{28,16},{1,13},{... | collective-permute-start | bytes 393224 | tf_op jit(solution)/shard_map/ppermute | solution.py:35
  27.5 32.0 %collective-permute-start.3 = (bf16[2,128,256]{2,1,0:T(8,128)(2,1)S(1)}, bf16[2,128,256]{2,1,0:T(8,128)(2,1)}, u32[]{:S(2)}, u32[]{:S(2)}) collective-permute-start(bf16[2,128,256]{2,1,0:T(8,128)(2,1)S(1)} %bitcast.263), channel_id=1, source_target_pairs={{0,16},{4,20},{8,24},{12,28},{16,0},{20,4},{24,8},{28,12},{1,17},{... | collective-permute-start | bytes 393224 | tf_op jit(solution)/shard_map/ppermute | solution.py:35
  30.5 32.1 %collective-permute-start.4 = (bf16[2,128,256]{2,1,0:T(8,128)(2,1)S(1)}, bf16[2,128,256]{2,1,0:T(8,128)(2,1)S(1)}, u32[]{:S(2)}, u32[]{:S(2)}) collective-permute-start(bf16[2,128,256]{2,1,0:T(8,128)(2,1)S(1)} %bitcast.262), channel_id=1, source_target_pairs={{0,20},{4,16},{8,28},{12,24},{16,4},{20,0},{24,12},{28,8},{1,21},{... | collective-permute-start | bytes 393224 | tf_op jit(solution)/shard_map/ppermute | solution.py:35
  32.5 30.2 %collective-permute-start.5 = (bf16[2,128,256]{2,1,0:T(8,128)(2,1)S(1)}, bf16[2,128,256]{2,1,0:T(8,128)(2,1)S(1)}, u32[]{:S(2)}, u32[]{:S(2)}) collective-permute-start(bf16[2,128,256]{2,1,0:T(8,128)(2,1)S(1)} %bitcast.264), channel_id=1, source_target_pairs={{0,24},{4,28},{8,16},{12,20},{16,8},{20,12},{24,0},{28,4},{1,25},{... | collective-permute-start | bytes 393224 | tf_op jit(solution)/shard_map/ppermute | solution.py:35
  39.4 23.3 %collective-permute-start.6 = (bf16[2,128,256]{2,1,0:T(8,128)(2,1)S(1)}, bf16[2,128,256]{2,1,0:T(8,128)(2,1)S(1)}, u32[]{:S(2)}, u32[]{:S(2)}) collective-permute-start(bf16[2,128,256]{2,1,0:T(8,128)(2,1)S(1)} %bitcast.261), channel_id=1, source_target_pairs={{0,28},{4,24},{8,20},{12,16},{16,12},{20,8},{24,4},{28,0},{1,29},{... | collective-permute-start | bytes 393224 | tf_op jit(solution)/shard_map/ppermute | solution.py:35
  66.9 1.7 copy-start.1
  72.5 44.3 %copy-start.20 = (s32[1,1,4]{2,1,0:T(1,128)S(1)}, s32[1,1,4]{2,1,0:T(1,128)}, u32[]{:S(2)}) copy-start(s32[1,1,4]{2,1,0:T(1,128)} %param.20) | copy-start | bytes 52
  72.5 47.6 %copy-start.18 = (bf16[1,1,16,121]{3,2,1,0:T(8,128)(2,1)S(1)}, bf16[1,1,16,121]{3,2,1,0:T(8,128)(2,1)}, u32[]{:S(2)}) copy-start(bf16[1,1,16,121]{3,2,1,0:T(8,128)(2,1)} %param.25) | copy-start | bytes 11620
  72.5 47.8 %copy-start.19 = (s32[1,1,4,4]{3,2,1,0:T(4,128)S(1)}, s32[1,1,4,4]{3,2,1,0:T(4,128)}, u32[]{:S(2)}) copy-start(s32[1,1,4,4]{3,2,1,0:T(4,128)} %param.24) | copy-start | bytes 196
  73.2 65.3 %all-gather.5.cloned.1.call-start = ((), (), s32[]{:S(2)}) async-start(), calls=%async_computation.2 | async-start | bytes 2621440 | tf_op jit(solution)/shard_map/all_gather | solution.py:115
  161.7 1.1 copy-start.15
  161.7 1.5 copy-start.14
  162.7 1.1 copy-start.13
  163.1 1.1 copy-start.12
  163.8 1.1 copy-start.11
  164.2 1.1 copy-start.10
  164.9 1.1 copy-start.9
  165.3 1.1 copy-start.8
  165.8 1.1 copy-start.7
  166.4 1.1 copy-start.6
  166.9 1.1 copy-start.5
  167.5 1.1 copy-start.4
  167.9 1.1 copy-start.3
  170.3 1.0 copy-start.16
  170.3 1.2 copy-start.17
  170.7 2.0 %copy-start.2 = (f32[128,2048]{1,0:T(8,128)S(1)}, f32[128,2048]{1,0:T(8,128)}, u32[]{:S(2)}) copy-start(f32[128,2048]{1,0:T(8,128)} %all-gather.3.cloned.1.call-done) | copy-start | bytes 3145732
Sparse Core Ops, SparseCore 0:
  73.3 41.2 all-gather.2
  116.9 21.5 all-gather.4
